TPU v7x, 32 devices: a whole 2x2x4 slice. The times are simulated.
32 devices in a mesh: groups: 2 (over y), seq: 4 (over z), tensor: 4 (over x, core).
Axes of the slice: x: 2, y: 2, z: 4, core: 2. Of those that a mesh axis runs over, the one named last changes fastest.
Arguments:
- x_in: bfloat16 [4096, 5120], P(('groups', 'seq'), 'tensor'), parts along dimension 0, may hold values from -6 to 6
- z_gate: bfloat16 [4096, 5120], P(('groups', 'seq'), 'tensor'), parts along dimension 0, may hold values from -32 to 32
- bc_in: bfloat16 [4096, 256], P(('groups', 'seq')), parts along dimension 0, may hold values from -6 to 6
- step_size: float32 [80, 4096], P('tensor', ('groups', 'seq')), parts along dimension 1, may hold values from 0 to 0.4
- log_keep: float32 [80, 4096], P('tensor', ('groups', 'seq')), parts along dimension 1, may hold values from -1 to 0
- skip_gain: float32 [80], P('tensor'), may hold values from 0.5 to 2
- conv_x: bfloat16 [4, 5120], P(None, 'tensor'), may hold values from -3 to 3
- conv_bc: bfloat16 [4, 256], replicated, may hold values from -3 to 3
- norm_gain: float32 [5120], P('tensor'), may hold values from 0.1 to 1.9
- seg_ends: int32 [1024], P(('groups', 'seq')), parts along dimension 0, may hold values from 0 to 2047, as said below
- pool_query: bfloat16 [320, 5120], P(('groups', 'seq'), 'tensor'), parts along dimension 0, may hold values from -64 to 64
- pool_start: int32 [320], P(('groups', 'seq')), parts along dimension 0, may hold values from 0 to 255, as said below
- pool_stop: int32 [320], P(('groups', 'seq')), parts along dimension 0, may hold values from 64 to 512
Outputs:
- mixed_seq: bfloat16 [4096, 5120], P(('groups', 'seq'), 'tensor'), parts along dimension 0
- pooled: float32 [320, 5120], P(('groups', 'seq'), 'tensor'), parts along dimension 0
There are 2 independent parts, one for each index of `groups`. A program takes and returns all parts, laid end to end along the dimension named above; an argument that names none is the same for every part. Nothing has to cross between parts.
Inputs may be any that keep to these rules, and one draw needn't show every extreme that they name: The tokens fall into blocks of 512; block b holds exactly the 128 segment ends seg_ends[b * 128] to seg_ends[(b + 1) * 128 - 1], strictly increasing. pool_start < pool_stop for every pooled row.
All inputs are finite; a program needn't handle non-finite values.
Results may differ from a plain program's by a relative error of at most 0.039.
Values may be sent and summed in bfloat16 or wider, within the bound.
No kernel may reach another device: no remote copies, remote signals or barrier semaphores. Data moves between devices by JAX's collectives and lax.ppermute only.
A program may use at most 64 MiB of HBM per device.

v0:
```python
import math
import jax
import jax.numpy as jnp
from jax import lax
from jax.sharding import PartitionSpec as P

STRETCH = 256
POOL_HEADS = 32
EPSILON = 1e-05
MASKED = -1e30


def passed_along(value, axis, steps):
    count = lax.axis_size(axis)
    leading, last = (max(0, -steps), min(count, count - steps))
    return lax.ppermute(value, axis, [(source, source + steps) for source in range(leading, last)])


def prefix(part, axis, combine, identity):
    place = lax.axis_index(axis)
    gathered = jax.tree.map(lambda a: lax.all_gather(a, axis), part)
    state = jax.tree.map(lambda a, e: jnp.zeros_like(a) + jnp.asarray(e, a.dtype), part, identity)

    def one(lap, state):
        return combine(
            state, jax.tree.map(lambda a: lax.dynamic_index_in_dim(a, lap, 0, False), gathered)
        )

    return lax.fori_loop(0, place, one, state)


def silu_act(values):
    return values / (1.0 + jnp.exp(-values))


def causal_conv(before, current, weights):
    kernel_width = weights.shape[0]
    length = current.shape[0]
    padded = jnp.concatenate([before, current], axis=0)
    summed = jnp.zeros(current.shape, jnp.float32)
    for offset in range(kernel_width):
        summed = summed + padded[offset : offset + length].astype(jnp.float32) * weights[
            offset
        ].astype(jnp.float32)
    return silu_act(summed).astype(jnp.bfloat16)


def stretch_local(x_block, b_block, c_block, step_block, keep_block):
    block_len = x_block.shape[0]
    cumul_keep = jnp.cumsum(keep_block, axis=1)
    lower_mask = lax.broadcasted_iota(jnp.int32, (block_len, block_len), 0) >= lax.broadcasted_iota(
        jnp.int32, (block_len, block_len), 1
    )
    inner_prod = jnp.einsum("is,js->ij", c_block, b_block, preferred_element_type=jnp.float32)
    spread = cumul_keep[:, :, None] - cumul_keep[:, None, :]
    decay_mask = jnp.where(lower_mask[None], jnp.exp(jnp.where(lower_mask[None], spread, 0.0)), 0.0)
    mixing = (decay_mask * inner_prod[None] * step_block[:, None, :]).astype(jnp.bfloat16)
    intra_part = jnp.einsum("hij,jhp->ihp", mixing, x_block, preferred_element_type=jnp.float32)
    tail_weight = jnp.exp(cumul_keep[:, -1:] - cumul_keep) * step_block
    weighted = (tail_weight.T[:, :, None] * x_block.astype(jnp.float32)).astype(jnp.bfloat16)
    stretch_state = jnp.einsum("jhp,js->hps", weighted, b_block, preferred_element_type=jnp.float32)
    return (intra_part, stretch_state, cumul_keep)


def combine(earlier, later):
    return (earlier[0] * jnp.exp(later[1])[:, None, None] + later[0], earlier[1] + later[1])


def read_state(c_block, state_in):
    state_high = state_in.astype(jnp.bfloat16)
    state_low = (state_in - state_high.astype(jnp.float32)).astype(jnp.bfloat16)
    high_part = jnp.einsum("is,hps->ihp", c_block, state_high, preferred_element_type=jnp.float32)
    low_part = jnp.einsum("is,hps->ihp", c_block, state_low, preferred_element_type=jnp.float32)
    return high_part + low_part


def local(
    x_in,
    z_gate,
    bc_in,
    step_size,
    log_keep,
    skip_gain,
    conv_x,
    conv_bc,
    norm_gain,
    seg_ends,
    pool_query,
    pool_start,
    pool_stop,
):
    tok_rows = x_in.shape[0]
    channels = x_in.shape[1]
    heads_local = step_size.shape[0]
    head_width = channels // heads_local
    state_width = bc_in.shape[1] // 2
    rim_rows = conv_x.shape[0] - 1
    edge_rows = jnp.concatenate([x_in[tok_rows - rim_rows :], bc_in[tok_rows - rim_rows :]], axis=1)
    before = passed_along(edge_rows, "seq", 1)
    x_conv = causal_conv(before[:, :channels], x_in, conv_x)
    bc_conv = causal_conv(before[:, channels:], bc_in, conv_bc)
    b_mat = bc_conv[:, :state_width]
    c_mat = bc_conv[:, state_width:]
    x_heads = x_conv.reshape(tok_rows, heads_local, head_width)
    stretch_count = tok_rows // STRETCH
    entry_state = jnp.zeros((heads_local, head_width, state_width), jnp.float32)
    decay_total = jnp.zeros((heads_local,), jnp.float32)
    saved_parts = []
    for block_index in range(stretch_count):
        first_row = block_index * STRETCH
        last_row = first_row + STRETCH
        intra_part, stretch_state, cumul_keep = stretch_local(
            x_heads[first_row:last_row],
            b_mat[first_row:last_row],
            c_mat[first_row:last_row],
            step_size[:, first_row:last_row],
            log_keep[:, first_row:last_row],
        )
        saved_parts.append((intra_part, cumul_keep, entry_state, decay_total))
        entry_state = jnp.exp(cumul_keep[:, -1])[:, None, None] * entry_state + stretch_state
        decay_total = decay_total + cumul_keep[:, -1]
    incoming, unused = prefix(
        (entry_state, decay_total),
        "seq",
        combine,
        (jnp.zeros_like(entry_state), jnp.zeros_like(decay_total)),
    )
    pieces_out = []
    for block_index in range(stretch_count):
        intra_part, cumul_keep, entry_part, decay_part = saved_parts[block_index]
        first_row = block_index * STRETCH
        state_in = entry_part + jnp.exp(decay_part)[:, None, None] * incoming
        from_state = read_state(c_mat[first_row : first_row + STRETCH], state_in)
        pieces_out.append(intra_part + jnp.exp(cumul_keep).T[:, :, None] * from_state)
    ssd_out = jnp.concatenate(pieces_out, axis=0) + skip_gain[None, :, None] * x_heads.astype(
        jnp.float32
    )
    gated = ssd_out.reshape(tok_rows, channels) * silu_act(z_gate.astype(jnp.float32))
    square_sum = lax.psum(jnp.sum(gated * gated, axis=1), "tensor")
    width_all = channels * lax.axis_size("tensor")
    mixed_seq = (
        gated * lax.rsqrt(square_sum / width_all + EPSILON)[:, None] * norm_gain[None, :]
    ).astype(jnp.bfloat16)
    local_ends = seg_ends - lax.axis_index("seq") * tok_rows
    summaries = jnp.take(mixed_seq, local_ends, axis=0)
    pool_heads_local = POOL_HEADS // lax.axis_size("tensor")
    pool_width = channels // pool_heads_local
    scale_factor = 1.0 / math.sqrt(pool_width)
    pools_local = pool_query.shape[0]
    queries = pool_query.reshape(pools_local, pool_heads_local, pool_width)
    piece = lax.all_gather(summaries, "seq", axis=0, tiled=True)
    peak = jnp.full((pool_heads_local, pools_local), MASKED, jnp.float32)
    numer = jnp.zeros((pools_local, pool_heads_local, pool_width), jnp.float32)
    count = piece.shape[0]
    seg_index = lax.iota(jnp.int32, count)
    inside = (seg_index[None, :] >= pool_start[:, None]) & (seg_index[None, :] < pool_stop[:, None])
    keys_block = piece.reshape(count, pool_heads_local, pool_width)
    logits = (
        jnp.einsum("pad,rad->apr", queries, keys_block, preferred_element_type=jnp.float32)
        * scale_factor
    )
    logits = jnp.where(inside[None], logits, MASKED)
    new_peak = jnp.maximum(peak, jnp.max(logits, axis=2))
    expo = jnp.where(inside[None], jnp.exp(logits - new_peak[:, :, None]), 0.0)
    rescale = jnp.exp(peak - new_peak)
    denom = jnp.sum(expo, axis=2)
    numer = numer * rescale.T[:, :, None] + jnp.einsum(
        "apr,rad->pad", expo.astype(jnp.bfloat16), keys_block, preferred_element_type=jnp.float32
    )
    peak, denom, numer = (new_peak, denom, numer)
    pooled = (numer / denom.T[:, :, None]).reshape(pools_local, channels)
    return (mixed_seq, pooled)


def solution(mesh):
    in_specs = (
        P(("groups", "seq"), "tensor"),
        P(("groups", "seq"), "tensor"),
        P(("groups", "seq"), None),
        P("tensor", ("groups", "seq")),
        P("tensor", ("groups", "seq")),
        P("tensor"),
        P(None, "tensor"),
        P(),
        P("tensor"),
        P(("groups", "seq")),
        P(("groups", "seq"), "tensor"),
        P(("groups", "seq")),
        P(("groups", "seq")),
    )
    out_specs = (P(("groups", "seq"), "tensor"), P(("groups", "seq"), "tensor"))
    return jax.shard_map(local, mesh=mesh, in_specs=in_specs, out_specs=out_specs, check_vma=False)
```

profile of v0, /device:TPU:0, one launch (start us, length us, event | category | flops | bytes accessed | tf_op | source)
XLA Modules:
  0.0 157.4 jit_solution(5044019205403970520)
XLA Ops:
  7.2 0.7 slice.120
  7.9 0.7 slice.121
  8.7 5.0 %collective-permute-start = (bf16[3,1536]{1,0:T(4,128)(2,1)S(1)}, bf16[3,1536]{1,0:T(4,128)(2,1)S(1)}, u32[]{:S(2)}, u32[]{:S(2)}) collective-permute-start(bf16[3,1536]{1,0:T(4,128)(2,1)S(1)} %pad_maximum_fusion.2), channel_id=1, source_target_pairs={{0,4},{4,8},{8,12},{1,5},{5,9},{9,13},{2,6},{6,10},{10,14},{3,7},{... | collective-permute-start | bytes 27656 | tf_op jit(solution)/shard_map/ppermute | solution.py:16
  13.6 0.8 fusion.71
  16.3 0.8 slice_convert_fusion.3
  17.2 0.8 slice_reduce_fusion.2
  18.5 1.5 fusion.70
  19.9 0.9 convert_reduce_fusion.3
  21.5 4.0 %divide_convert_fusion = bf16[512,1280]{1,0:T(8,128)(2,1)S(1)} fusion(bf16[512,1280]{1,0:T(8,128)(2,1)} %param.15, bf16[3,1280]{1,0:T(4,128)(2,1)S(1)} %slice.158, f32[1280]{0:T(1024)S(1)} %get-tuple-element.52, f32[1280]{0:T(1024)S(1)} %get-tuple-element.53, f32[1280]{0:T(1024)S(1)} %get-tuple-element.51, f32[1280]{0:T(1024)S(1)} %get-tuple-element.50), kind=kLoop, calls=%fused_computation.25 | loop fusion | flops 15728640 | bytes 2649600 | tf_op jit(solution)/shard_map/convert_element_type | solution.py:45
  26.1 1.9 %divide_convert_fusion.1 = bf16[512,256]{1,0:T(8,128)(2,1)S(1)} fusion(bf16[512,256]{1,0:T(8,128)(2,1)} %param.17, bf16[3,256]{1,0:T(4,128)(2,1)S(1)} %slice.165, f32[256]{0:T(256)S(1)} %bitcast.90, f32[256]{0:T(256)S(1)} %bitcast.91, f32[256]{0:T(256)S(1)} %bitcast.89, f32[256]{0:T(256)S(1)} %bitcast.88), kind=kLoop, calls=%fused_computation.59 | loop fusion | flops 3145728 | bytes 529920 | tf_op jit(solution)/shard_map/convert_element_type | solution.py:45
  28.0 1.1 convolution_add_fusion.3
  29.1 1.9 %convolution_add_fusion.2 = f32[20,64,128]{2,1,0:T(8,128)} fusion(bf16[256,20,64]{0,2,1:T(8,128)(2,1)S(1)} %bitcast.75, f32[256,20]{0,1:T(8,128)} %get-tuple-element.72, f32[20,64,128]{2,1,0:T(8,128)S(1)} %convolution_add_fusion.3, f32[20]{0:T(128)} %exp.65, bf16[512,256]{1,0:T(8,128)(2,1)S(1)} %divide_convert_fusion.1), kind=kOutput, calls=%fused_computation.43 | convolution fusion | flops 85196800 | bytes 2052176 | tf_op jit(solution)/shard_map/jhp,js->hps/dot_general | solution.py:61
  31.1 1.2 dynamic-slice
  33.0 0.9 dynamic-update-slice
  33.8 10.1 %all-reduce = f32[80]{0:T(128)S(1)} all-reduce(f32[80]{0:T(128)S(1)} %dynamic-update-slice), channel_id=2, replica_groups=mesh['groups'=2,'seq'=4,'tensor'=4] {'seq'}, use_global_device_ids=true, to_apply=%add | all-reduce | flops 80 | bytes 640
  44.1 0.7 mul.319
  46.5 3.7 %fusion.18 = f32[256,20,64]{0,2,1:T(8,128)} fusion(bf16[256,20,64]{0,2,1:T(8,128)(2,1)S(1)} %bitcast.78, f32[20,256]{1,0:T(8,128)} %get-tuple-element.70, f32[256,256]{1,0:T(8,128)S(1)} %fusion.57, f32[20,256]{1,0:T(8,128)} %bitcast.81, pred[256,256]{1,0:T(8,128)(4,1)S(1)} %iota_compare_fusion), kind=kOutput, calls=%fused_computation.31 | convolution fusion | flops 175636480 | bytes 2334720 | tf_op jit(solution)/shard_map/hij,jhp->ihp/dot_general | solution.py:58
  50.3 2.9 %fusion.17 = f32[256,20,64]{0,2,1:T(8,128)} fusion(bf16[256,20,64]{0,2,1:T(8,128)(2,1)S(1)} %bitcast.76, f32[20,256]{1,0:T(8,128)S(1)} %copy-done.11, f32[256,256]{1,0:T(8,128)S(1)} %fusion.53, f32[20,256]{1,0:T(8,128)S(1)} %bitcast.84, pred[256,256]{1,0:T(8,128)(4,1)S(1)} %iota_compare_fusion), kind=kOutput, calls=%fused_computation.30 | convolution fusion | flops 175636480 | bytes 2334720 | tf_op jit(solution)/shard_map/hij,jhp->ihp/dot_general | solution.py:58
  53.1 33.0 %all-gather.7.cloned.1.call-done = f32[80,64,128]{2,1,0:T(8,128)} async-done(((f32[20,64,128]{2,1,0:T(8,128)}), f32[80,64,128]{2,1,0:T(8,128)}) %all-gather.7.cloned.1.call-update) | async-done | bytes 2621456 | tf_op jit(solution)/shard_map/all_gather | solution.py:21
  87.6 1.4 fusion.21
  89.0 2.8 %copy.40 = f32[256,1280]{1,0:T(8,128)} copy(f32[256,1280]{0,1:T(8,128)} %bitcast.73) | data formatting | bytes 2621440 | tf_op jit(solution)/shard_map/concatenate | solution.py:135
  92.2 0.9 copy-done.2
  93.1 1.4 fusion.22
  94.6 2.9 %copy.41 = f32[256,1280]{1,0:T(8,128)} copy(f32[256,1280]{0,1:T(8,128)} %bitcast.72) | data formatting | bytes 2621440 | tf_op jit(solution)/shard_map/concatenate | solution.py:135
  97.5 4.2 %multiply_reduce_fusion = (f32[512]{0:T(512)S(1)}, f32[512,1280]{1,0:T(8,128)}) fusion(bf16[512,1280]{1,0:T(8,128)(2,1)} %param.16, bf16[512,1280]{1,0:T(8,128)(2,1)S(1)} %divide_convert_fusion, f32[1280]{0:T(1024)S(1)} %copy-done.10, f32[256,1280]{1,0:T(8,128)} %copy.41, f32[256,1280]{1,0:T(8,128)S(1)} %copy-done.1), kind=kLoop, calls=%fused_computation.14 | loop fusion | flops 7208448 | bytes 7871488 | tf_op jit(solution)/shard_map/reduce_sum | solution.py:139
  101.7 6.4 %psum.7 = f32[512]{0:T(512)S(1)} all-reduce(f32[512]{0:T(512)S(1)} %get-tuple-element.66), channel_id=1, replica_groups=mesh['groups'=2,'seq'=4,'tensor'=4] {'tensor'}, use_global_device_ids=true, to_apply=%region_7.8 | all-reduce | flops 512 | bytes 4096 | tf_op jit(solution)/shard_map/psum | solution.py:139
  108.1 2.0 %multiply_convert_fusion.4 = bf16[512,1280]{1,0:T(8,128)(2,1)S(1)} fusion(f32[512,1280]{1,0:T(8,128)} %get-tuple-element.67, f32[1280]{0:T(1024)S(1)} %copy-done.12, f32[512]{0:T(512)S(1)} %add_rsqrt_fusion), kind=kLoop, calls=%fused_computation.13 | loop fusion | flops 1966080 | bytes 3939328 | tf_op jit(solution)/shard_map/convert_element_type | solution.py:143
  110.2 0.9 gather_fusion
  111.1 0.8 broadcast_select_fusion
  112.3 34.4 %all-gather.5.cloned.1.call-done = bf16[512,1280]{1,0:T(8,128)(2,1)} async-done(((bf16[128,1280]{1,0:T(8,128)(2,1)}), bf16[512,1280]{1,0:T(8,128)(2,1)}) %all-gather.5.cloned.1.call-update) | async-done | bytes 1310736 | tf_op jit(solution)/shard_map/all_gather | solution.py:151
  146.7 1.6 %copy.42 = bf16[512,1280]{0,1:T(8,128)(2,1)S(1)} copy(bf16[512,1280]{1,0:T(8,128)(2,1)} %all-gather.5.cloned.1.call-done) | data formatting | bytes 2621440 | tf_op jit(solution)/shard_map/all_gather | solution.py:151
  149.7 0.8 reshape.193
  (84 shorter events, 9.0 us)
Async XLA Ops:
  7.2 79.0 %all-gather.7.cloned.1.call-start = ((), (), s32[]{:S(2)}) async-start(), calls=%async_computation.1 | async-start | bytes 3276800 | tf_op jit(solution)/shard_map/all_gather | solution.py:21
  8.7 12.8 %collective-permute-start = (bf16[3,1536]{1,0:T(4,128)(2,1)S(1)}, bf16[3,1536]{1,0:T(4,128)(2,1)S(1)}, u32[]{:S(2)}, u32[]{:S(2)}) collective-permute-start(bf16[3,1536]{1,0:T(4,128)(2,1)S(1)} %pad_maximum_fusion.2), channel_id=1, source_target_pairs={{0,4},{4,8},{8,12},{1,5},{5,9},{9,13},{2,6},{6,10},{10,14},{3,7},{... | collective-permute-start | bytes 27656 | tf_op jit(solution)/shard_map/ppermute | solution.py:16
  15.3 6.1 %copy-start.4 = (f32[3,8,2,128]{3,1,2,0:T(8,128)}, f32[3,8,2,128]{3,1,2,0:T(8,128)S(1)}, u32[]{:S(2)}) copy-start(f32[3,8,2,128]{3,1,2,0:T(8,128)S(1)} %copy.45) | copy-start | bytes 73732
  16.3 5.1 %copy-start.5 = (f32[3,8,2,128]{3,1,2,0:T(8,128)}, f32[3,8,2,128]{3,1,2,0:T(8,128)S(1)}, u32[]{:S(2)}) copy-start(f32[3,8,2,128]{3,1,2,0:T(8,128)S(1)} %copy.46) | copy-start | bytes 73732
  31.0 115.7 %all-gather.5.cloned.1.call-start = ((), (), s32[]{:S(2)}) async-start(), calls=%async_computation | async-start | bytes 1638400 | tf_op jit(solution)/shard_map/all_gather | solution.py:151
  46.5 3.7 %copy-start.6 = (f32[3,8,2,128]{3,1,2,0:T(8,128)S(1)}, f32[3,8,2,128]{3,1,2,0:T(8,128)}, u32[]{:S(2)}) copy-start(f32[3,8,2,128]{3,1,2,0:T(8,128)} %copy-done.5) | copy-start | bytes 73732
  46.5 3.7 %copy-start.11 = (f32[20,256]{1,0:T(8,128)S(1)}, f32[20,256]{1,0:T(8,128)}, u32[]{:S(2)}) copy-start(f32[20,256]{1,0:T(8,128)} %get-tuple-element.73) | copy-start | bytes 61444
  86.3 0.7 copy-start.9
  86.3 1.3 copy-start.3
  87.6 4.2 %copy-start.13 = (f32[20]{0:T(128)S(1)}, f32[20]{0:T(128)}, u32[]{:S(2)}) copy-start(f32[20]{0:T(128)} %get-tuple-element.84) | copy-start | bytes 244
  89.0 3.2 %copy-start.8 = (f32[256,20]{0,1:T(8,128)S(1)}, f32[256,20]{0,1:T(8,128)}, u32[]{:S(2)}) copy-start(f32[256,20]{0,1:T(8,128)} %get-tuple-element.76) | copy-start | bytes 61444
  91.8 1.3 copy-start.2
  94.6 2.9 %copy-start.1 = (f32[256,1280]{1,0:T(8,128)S(1)}, f32[256,1280]{1,0:T(8,128)}, u32[]{:S(2)}) copy-start(f32[256,1280]{1,0:T(8,128)} %copy.40) | copy-start | bytes 3932164
  94.6 2.9 %copy-start.10 = (f32[1280]{0:T(1024)S(1)}, f32[1280]{0:T(1024)}, u32[]{:S(2)}) copy-start(f32[1280]{0:T(1024)} %mul.320) | copy-start | bytes 15364
  97.5 10.6 %copy-start.12 = (f32[1280]{0:T(1024)S(1)}, f32[1280]{0:T(1024)}, u32[]{:S(2)}) copy-start(f32[1280]{0:T(1024)} %param.23) | copy-start | bytes 15364
  110.1 38.2 %copy-start = (bf16[512,1280]{1,0:T(8,128)(2,1)}, bf16[512,1280]{1,0:T(8,128)(2,1)S(1)}, u32[]{:S(2)}) copy-start(bf16[512,1280]{1,0:T(8,128)(2,1)S(1)} %multiply_convert_fusion.4) | copy-start | bytes 3932164
  110.2 1.8 %copy-start.7 = (bf16[40,1280]{1,0:T(8,128)(2,1)S(1)}, bf16[40,1280]{1,0:T(8,128)(2,1)}, u32[]{:S(2)}) copy-start(bf16[40,1280]{1,0:T(8,128)(2,1)} %param.25) | copy-start | bytes 307204
  110.2 2.0 %copy-start.14 = (s32[40]{0:T(128)S(1)}, s32[40]{0:T(128)}, u32[]{:S(2)}) copy-start(s32[40]{0:T(128)} %param.27) | copy-start | bytes 484
  110.2 2.0 %copy-start.15 = (s32[40]{0:T(128)S(1)}, s32[40]{0:T(128)}, u32[]{:S(2)}) copy-start(s32[40]{0:T(128)} %param.26) | copy-start | bytes 484
Sparse Core Ops, SparseCore 0:
  31.1 55.0 all-gather.6
  112.1 34.5 all-gather.4
where the time goes:
time: 158 us; the launch traced here: 157 us
  waiting for transfers between devices  67.5 us (43%)
  other arithmetic  20 us (13%)
  local copies, waits for them, and re-layouts  18.7 us (12%)
  blocking collectives  16.5 us (10%)
  between operations  15.1 us (10%)
  matrix products  14.5 us (9%)
  starting transfers between devices  5.04 us (3%)
    all_gather x1, waiting for transfers between devices, local(): piece = lax.all_gather(summaries, 'seq', axis=0, tiled=True)  34.4 us
    all_gather x1, waiting for transfers between devices, prefix(): gathered = jax.tree.map(lambda a: lax.all_gather(a, axis), part)  33 us
    unnamed x1, blocking collectives  10.1 us
    dot_general x2, matrix products, stretch_local(): jnp.einsum('hij,jhp->ihp', mixing, x_block, preferred_element_type=jnp.fl...  6.59 us
    psum x1, blocking collectives, local(): square_sum = lax.psum(jnp.sum(gated * gated, axis=1), 'tensor')  6.37 us
    convert_element_type x2, other arithmetic, causal_conv(): return silu_act(summed).astype(jnp.bfloat16)  5.91 us
    concatenate x2, local copies, waits for them, and re-layouts, local(): jnp.concatenate(pieces_out, axis=0)  5.7 us
    ppermute x1, starting transfers between devices, passed_along(): lax.ppermute(value, axis, [(source, source + steps) for source in range(l...  4.96 us
  transfers between devices with their start and end apart: 3, of which 2 were waited for; matrix products, arithmetic and copies ran while one was open for 12% of the time, Pallas kernels for 0%

commit v1 on v0

--- a/solution.py
+++ b/solution.py
@@ -148,7 +148,16 @@
     scale_factor = 1.0 / math.sqrt(pool_width)
     pools_local = pool_query.shape[0]
     queries = pool_query.reshape(pools_local, pool_heads_local, pool_width)
-    piece = lax.all_gather(summaries, "seq", axis=0, tiled=True)
+    ways = lax.axis_size("seq")
+    up = [(d, (d + 1) % ways) for d in range(ways)]
+    down = [(d, (d - 1) % ways) for d in range(ways)]
+    earlier_2, later_2 = ([summaries], [summaries])
+    for _ in range(ways // 2):
+        earlier_2.append(lax.ppermute(earlier_2[-1], "seq", up))
+    for _ in range((ways - 1) // 2):
+        later_2.append(lax.ppermute(later_2[-1], "seq", down))
+    line = jnp.concatenate([*earlier_2[::-1], *later_2[1:]], axis=0)
+    piece = jnp.roll(line, (lax.axis_index("seq") - ways // 2) * summaries.shape[0], axis=0)
     peak = jnp.full((pool_heads_local, pools_local), MASKED, jnp.float32)
     numer = jnp.zeros((pools_local, pool_heads_local, pool_width), jnp.float32)
     count = piece.shape[0]

time: 158 us -> 149 us (0.943)
  waiting for transfers between devices: 67.5 us -> 54.8 us
  starting transfers between devices: 5.04 us -> 9.58 us
    all_gather x1 -> x0, waiting for transfers between devices: 34.4 us -> none  [local(): piece = lax.all_gather(summaries, 'seq', axis=0, tiled=True)]
    ppermute x0 -> x3, waiting for transfers between devices: none -> 21.7 us  [the longest x2 19.3 us: local(): earlier_2.append(lax.ppermute(earlier_2[-1], 'seq', up))]
    ppermute x0 -> x3, starting transfers between devices: none -> 4.59 us  [the longest x1 3.87 us: local(): later_2.append(lax.ppermute(later_2[-1], 'seq', down))]
    all_gather x1 -> x0, local copies, waits for them, and re-layouts: 1.6 us -> none  [local(): piece = lax.all_gather(summaries, 'seq', axis=0, tiled=True)]
    unnamed x39 -> x44, local copies, waits for them, and re-layouts: 4.11 us -> 4.22 us
  transfers between devices with their start and end apart: 3 -> 5, of which waited for: 2 -> 4; matrix products, arithmetic and copies ran while one was open for 12% -> 13% of each run, Pallas kernels for 0% -> 0%
where the time goes in v1:
time: 149 us; the launch traced here: 148 us
  waiting for transfers between devices  54.8 us (37%)
  other arithmetic  19.5 us (13%)
  local copies, waits for them, and re-layouts  18 us (12%)
  blocking collectives  16.5 us (11%)
  between operations  15.2 us (10%)
  matrix products  14.5 us (10%)
  starting transfers between devices  9.58 us (6%)
    all_gather x1, waiting for transfers between devices, prefix(): gathered = jax.tree.map(lambda a: lax.all_gather(a, axis), part)  33.1 us
    ppermute x2, waiting for transfers between devices, local(): earlier_2.append(lax.ppermute(earlier_2[-1], 'seq', up))  19.3 us
    unnamed x1, blocking collectives  10.1 us
    dot_general x2, matrix products, stretch_local(): jnp.einsum('hij,jhp->ihp', mixing, x_block, preferred_element_type=jnp.fl...  6.59 us
    psum x1, blocking collectives, local(): square_sum = lax.psum(jnp.sum(gated * gated, axis=1), 'tensor')  6.37 us
    convert_element_type x2, other arithmetic, causal_conv(): return silu_act(summed).astype(jnp.bfloat16)  5.91 us
    concatenate x2, local copies, waits for them, and re-layouts, local(): jnp.concatenate(pieces_out, axis=0)  5.7 us
    ppermute x1, starting transfers between devices, passed_along(): lax.ppermute(value, axis, [(source, source + steps) for source in range(l...  4.96 us
  transfers between devices with their start and end apart: 5, of which 4 were waited for; matrix products, arithmetic and copies ran while one was open for 13% of the time, Pallas kernels for 0%

profile of v1, /device:TPU:0, one launch (start us, length us, event | category | flops | bytes accessed | tf_op | source)
XLA Modules:
  0.0 148.1 jit_solution(9848683213221025026)
XLA Ops:
  7.2 0.7 slice.120
  8.7 5.0 %collective-permute-start = (bf16[3,1536]{1,0:T(4,128)(2,1)S(1)}, bf16[3,1536]{1,0:T(4,128)(2,1)S(1)}, u32[]{:S(2)}, u32[]{:S(2)}) collective-permute-start(bf16[3,1536]{1,0:T(4,128)(2,1)S(1)} %pad_maximum_fusion.2), channel_id=1, source_target_pairs={{0,4},{4,8},{8,12},{1,5},{5,9},{9,13},{2,6},{6,10},{10,14},{3,7},{... | collective-permute-start | bytes 27656 | tf_op jit(solution)/shard_map/ppermute | solution.py:16
  13.6 0.8 fusion.71
  16.3 0.8 slice_convert_fusion.3
  17.2 0.8 slice_reduce_fusion.2
  18.5 1.5 fusion.70
  19.9 0.9 convert_reduce_fusion.3
  21.5 4.0 %divide_convert_fusion = bf16[512,1280]{1,0:T(8,128)(2,1)S(1)} fusion(bf16[512,1280]{1,0:T(8,128)(2,1)} %param.15, bf16[3,1280]{1,0:T(4,128)(2,1)S(1)} %slice.158, f32[1280]{0:T(1024)S(1)} %get-tuple-element.52, f32[1280]{0:T(1024)S(1)} %get-tuple-element.53, f32[1280]{0:T(1024)S(1)} %get-tuple-element.51, f32[1280]{0:T(1024)S(1)} %get-tuple-element.50), kind=kLoop, calls=%fused_computation.25 | loop fusion | flops 15728640 | bytes 2649600 | tf_op jit(solution)/shard_map/convert_element_type | solution.py:45
  26.1 1.9 %divide_convert_fusion.1 = bf16[512,256]{1,0:T(8,128)(2,1)S(1)} fusion(bf16[512,256]{1,0:T(8,128)(2,1)} %param.17, bf16[3,256]{1,0:T(4,128)(2,1)S(1)} %slice.165, f32[256]{0:T(256)S(1)} %bitcast.90, f32[256]{0:T(256)S(1)} %bitcast.91, f32[256]{0:T(256)S(1)} %bitcast.89, f32[256]{0:T(256)S(1)} %bitcast.88), kind=kLoop, calls=%fused_computation.59 | loop fusion | flops 3145728 | bytes 529920 | tf_op jit(solution)/shard_map/convert_element_type | solution.py:45
  28.0 1.1 convolution_add_fusion.3
  29.1 1.9 %convolution_add_fusion.2 = f32[20,64,128]{2,1,0:T(8,128)} fusion(bf16[256,20,64]{0,2,1:T(8,128)(2,1)S(1)} %bitcast.75, f32[256,20]{0,1:T(8,128)} %get-tuple-element.72, f32[20,64,128]{2,1,0:T(8,128)S(1)} %convolution_add_fusion.3, f32[20]{0:T(128)} %exp.65, bf16[512,256]{1,0:T(8,128)(2,1)S(1)} %divide_convert_fusion.1), kind=kOutput, calls=%fused_computation.43 | convolution fusion | flops 85196800 | bytes 2052176 | tf_op jit(solution)/shard_map/jhp,js->hps/dot_general | solution.py:61
  31.0 1.2 dynamic-slice
  32.9 0.9 dynamic-update-slice
  33.8 10.1 %all-reduce = f32[80]{0:T(128)S(1)} all-reduce(f32[80]{0:T(128)S(1)} %dynamic-update-slice), channel_id=2, replica_groups=mesh['groups'=2,'seq'=4,'tensor'=4] {'seq'}, use_global_device_ids=true, to_apply=%add | all-reduce | flops 80 | bytes 640
  44.0 0.7 mul.322
  46.5 3.7 %fusion.18 = f32[256,20,64]{0,2,1:T(8,128)} fusion(bf16[256,20,64]{0,2,1:T(8,128)(2,1)S(1)} %bitcast.78, f32[20,256]{1,0:T(8,128)} %get-tuple-element.70, f32[256,256]{1,0:T(8,128)S(1)} %fusion.57, f32[20,256]{1,0:T(8,128)} %bitcast.81, pred[256,256]{1,0:T(8,128)(4,1)S(1)} %iota_compare_fusion), kind=kOutput, calls=%fused_computation.31 | convolution fusion | flops 175636480 | bytes 2334720 | tf_op jit(solution)/shard_map/hij,jhp->ihp/dot_general | solution.py:58
  50.2 2.9 %fusion.17 = f32[256,20,64]{0,2,1:T(8,128)} fusion(bf16[256,20,64]{0,2,1:T(8,128)(2,1)S(1)} %bitcast.76, f32[20,256]{1,0:T(8,128)S(1)} %copy-done.11, f32[256,256]{1,0:T(8,128)S(1)} %fusion.53, f32[20,256]{1,0:T(8,128)S(1)} %bitcast.84, pred[256,256]{1,0:T(8,128)(4,1)S(1)} %iota_compare_fusion), kind=kOutput, calls=%fused_computation.30 | convolution fusion | flops 175636480 | bytes 2334720 | tf_op jit(solution)/shard_map/hij,jhp->ihp/dot_general | solution.py:58
  53.1 33.1 %all-gather.4.cloned.1.call-done = f32[80,64,128]{2,1,0:T(8,128)} async-done(((f32[20,64,128]{2,1,0:T(8,128)}), f32[80,64,128]{2,1,0:T(8,128)}) %all-gather.4.cloned.1.call-update) | async-done | bytes 2621456 | tf_op jit(solution)/shard_map/all_gather | solution.py:21
  87.6 1.4 fusion.21
  89.0 2.8 %copy.40 = f32[256,1280]{1,0:T(8,128)} copy(f32[256,1280]{0,1:T(8,128)} %bitcast.73) | data formatting | bytes 2621440 | tf_op jit(solution)/shard_map/concatenate | solution.py:135
  92.2 0.9 copy-done.2
  93.1 1.4 fusion.22
  94.6 2.9 %copy.41 = f32[256,1280]{1,0:T(8,128)} copy(f32[256,1280]{0,1:T(8,128)} %bitcast.72) | data formatting | bytes 2621440 | tf_op jit(solution)/shard_map/concatenate | solution.py:135
  97.5 4.2 %multiply_reduce_fusion = (f32[512]{0:T(512)S(1)}, f32[512,1280]{1,0:T(8,128)}) fusion(bf16[512,1280]{1,0:T(8,128)(2,1)} %param.16, bf16[512,1280]{1,0:T(8,128)(2,1)S(1)} %divide_convert_fusion, f32[1280]{0:T(1024)S(1)} %copy-done.10, f32[256,1280]{1,0:T(8,128)} %copy.41, f32[256,1280]{1,0:T(8,128)S(1)} %copy-done.1), kind=kLoop, calls=%fused_computation.14 | loop fusion | flops 7208448 | bytes 7871488 | tf_op jit(solution)/shard_map/reduce_sum | solution.py:139
  101.7 6.4 %psum.7 = f32[512]{0:T(512)S(1)} all-reduce(f32[512]{0:T(512)S(1)} %get-tuple-element.66), channel_id=1, replica_groups=mesh['groups'=2,'seq'=4,'tensor'=4] {'tensor'}, use_global_device_ids=true, to_apply=%region_7.8 | all-reduce | flops 512 | bytes 4096 | tf_op jit(solution)/shard_map/psum | solution.py:139
  108.1 2.0 %multiply_convert_fusion.4 = bf16[512,1280]{1,0:T(8,128)(2,1)S(1)} fusion(f32[512,1280]{1,0:T(8,128)} %get-tuple-element.67, f32[1280]{0:T(1024)S(1)} %copy-done.12, f32[512]{0:T(512)S(1)} %add_rsqrt_fusion), kind=kLoop, calls=%fused_computation.13 | loop fusion | flops 1966080 | bytes 3939328 | tf_op jit(solution)/shard_map/convert_element_type | solution.py:143
  110.2 0.9 gather_fusion
  111.9 11.1 %collective-permute-done.1 = bf16[128,1280]{1,0:T(8,128)(2,1)S(1)} collective-permute-done((bf16[128,1280]{1,0:T(8,128)(2,1)S(1)}, bf16[128,1280]{1,0:T(8,128)(2,1)S(1)}, u32[]{:S(2)}, u32[]{:S(2)}) %collective-permute-start.1) | collective-permute-done | bytes 327712 | tf_op jit(solution)/shard_map/ppermute | solution.py:156
  123.3 3.9 %collective-permute-start.3 = (bf16[128,1280]{1,0:T(8,128)(2,1)S(1)}, bf16[128,1280]{1,0:T(8,128)(2,1)S(1)}, u32[]{:S(2)}, u32[]{:S(2)}) collective-permute-start(bf16[128,1280]{1,0:T(8,128)(2,1)S(1)} %broadcast_select_fusion), channel_id=1, source_target_pairs={{0,12},{4,0},{8,4},{12,8},{1,13},{5,1},{9,5},{13,9},{2,14},{6,2},{... | collective-permute-start | bytes 983048 | tf_op jit(solution)/shard_map/ppermute | solution.py:158
  127.2 8.2 %collective-permute-done.2 = bf16[128,1280]{1,0:T(8,128)(2,1)S(1)} collective-permute-done((bf16[128,1280]{1,0:T(8,128)(2,1)S(1)}, bf16[128,1280]{1,0:T(8,128)(2,1)S(1)}, u32[]{:S(2)}, u32[]{:S(2)}) %collective-permute-start.2) | collective-permute-done | bytes 327712 | tf_op jit(solution)/shard_map/ppermute | solution.py:156
  135.6 2.4 %collective-permute-done.3 = bf16[128,1280]{1,0:T(8,128)(2,1)S(1)} collective-permute-done((bf16[128,1280]{1,0:T(8,128)(2,1)S(1)}, bf16[128,1280]{1,0:T(8,128)(2,1)S(1)}, u32[]{:S(2)}, u32[]{:S(2)}) %collective-permute-start.3) | collective-permute-done | bytes 327712 | tf_op jit(solution)/shard_map/ppermute | solution.py:158
  140.4 0.8 reshape.193
  (96 shorter events, 11.5 us)
Async XLA Ops:
  7.2 79.0 %all-gather.4.cloned.1.call-start = ((), (), s32[]{:S(2)}) async-start(), calls=%async_computation | async-start | bytes 3276800 | tf_op jit(solution)/shard_map/all_gather | solution.py:21
  8.7 12.8 %collective-permute-start = (bf16[3,1536]{1,0:T(4,128)(2,1)S(1)}, bf16[3,1536]{1,0:T(4,128)(2,1)S(1)}, u32[]{:S(2)}, u32[]{:S(2)}) collective-permute-start(bf16[3,1536]{1,0:T(4,128)(2,1)S(1)} %pad_maximum_fusion.2), channel_id=1, source_target_pairs={{0,4},{4,8},{8,12},{1,5},{5,9},{9,13},{2,6},{6,10},{10,14},{3,7},{... | collective-permute-start | bytes 27656 | tf_op jit(solution)/shard_map/ppermute | solution.py:16
  15.3 6.1 %copy-start.4 = (f32[3,8,2,128]{3,1,2,0:T(8,128)}, f32[3,8,2,128]{3,1,2,0:T(8,128)S(1)}, u32[]{:S(2)}) copy-start(f32[3,8,2,128]{3,1,2,0:T(8,128)S(1)} %copy.45) | copy-start | bytes 73732
  16.3 5.1 %copy-start.5 = (f32[3,8,2,128]{3,1,2,0:T(8,128)}, f32[3,8,2,128]{3,1,2,0:T(8,128)S(1)}, u32[]{:S(2)}) copy-start(f32[3,8,2,128]{3,1,2,0:T(8,128)S(1)} %copy.46) | copy-start | bytes 73732
  46.5 3.7 %copy-start.6 = (f32[3,8,2,128]{3,1,2,0:T(8,128)S(1)}, f32[3,8,2,128]{3,1,2,0:T(8,128)}, u32[]{:S(2)}) copy-start(f32[3,8,2,128]{3,1,2,0:T(8,128)} %copy-done.5) | copy-start | bytes 73732
  46.5 3.7 %copy-start.11 = (f32[20,256]{1,0:T(8,128)S(1)}, f32[20,256]{1,0:T(8,128)}, u32[]{:S(2)}) copy-start(f32[20,256]{1,0:T(8,128)} %get-tuple-element.73) | copy-start | bytes 61444
  86.3 0.7 copy-start.9
  86.3 1.3 copy-start.3
  87.6 4.2 %copy-start.13 = (f32[20]{0:T(128)S(1)}, f32[20]{0:T(128)}, u32[]{:S(2)}) copy-start(f32[20]{0:T(128)} %get-tuple-element.84) | copy-start | bytes 244
  89.0 3.2 %copy-start.8 = (f32[256,20]{0,1:T(8,128)S(1)}, f32[256,20]{0,1:T(8,128)}, u32[]{:S(2)}) copy-start(f32[256,20]{0,1:T(8,128)} %get-tuple-element.76) | copy-start | bytes 61444
  91.8 1.3 copy-start.2
  94.6 2.9 %copy-start.1 = (f32[256,1280]{1,0:T(8,128)S(1)}, f32[256,1280]{1,0:T(8,128)}, u32[]{:S(2)}) copy-start(f32[256,1280]{1,0:T(8,128)} %copy.40) | copy-start | bytes 3932164
  94.6 2.9 %copy-start.10 = (f32[1280]{0:T(1024)S(1)}, f32[1280]{0:T(1024)}, u32[]{:S(2)}) copy-start(f32[1280]{0:T(1024)} %mul.323) | copy-start | bytes 15364
  97.5 10.6 %copy-start.12 = (f32[1280]{0:T(1024)S(1)}, f32[1280]{0:T(1024)}, u32[]{:S(2)}) copy-start(f32[1280]{0:T(1024)} %param.23) | copy-start | bytes 15364
  110.1 25.4 %copy-start = (bf16[512,1280]{1,0:T(8,128)(2,1)}, bf16[512,1280]{1,0:T(8,128)(2,1)S(1)}, u32[]{:S(2)}) copy-start(bf16[512,1280]{1,0:T(8,128)(2,1)S(1)} %multiply_convert_fusion.4) | copy-start | bytes 3932164
  110.2 12.9 %copy-start.7 = (bf16[40,1280]{1,0:T(8,128)(2,1)S(1)}, bf16[40,1280]{1,0:T(8,128)(2,1)}, u32[]{:S(2)}) copy-start(bf16[40,1280]{1,0:T(8,128)(2,1)} %param.25) | copy-start | bytes 307204
  110.2 13.1 %copy-start.14 = (s32[40]{0:T(128)S(1)}, s32[40]{0:T(128)}, u32[]{:S(2)}) copy-start(s32[40]{0:T(128)} %param.27) | copy-start | bytes 484
  110.2 13.1 %copy-start.15 = (s32[40]{0:T(128)S(1)}, s32[40]{0:T(128)}, u32[]{:S(2)}) copy-start(s32[40]{0:T(128)} %param.26) | copy-start | bytes 484
  111.2 11.8 %collective-permute-start.1 = (bf16[128,1280]{1,0:T(8,128)(2,1)S(1)}, bf16[128,1280]{1,0:T(8,128)(2,1)S(1)}, u32[]{:S(2)}, u32[]{:S(2)}) collective-permute-start(bf16[128,1280]{1,0:T(8,128)(2,1)S(1)} %broadcast_select_fusion), channel_id=1, source_target_pairs={{0,4},{4,8},{8,12},{12,0},{1,5},{5,9},{9,13},{13,1},{2,6},{6,10},{... | collective-permute-start | bytes 983048 | tf_op jit(solution)/shard_map/ppermute | solution.py:156
  123.0 12.4 %collective-permute-start.2 = (bf16[128,1280]{1,0:T(8,128)(2,1)S(1)}, bf16[128,1280]{1,0:T(8,128)(2,1)S(1)}, u32[]{:S(2)}, u32[]{:S(2)}) collective-permute-start(bf16[128,1280]{1,0:T(8,128)(2,1)S(1)} %collective-permute-done.1), channel_id=1, source_target_pairs={{0,4},{4,8},{8,12},{12,0},{1,5},{5,9},{9,13},{13,1},{2,6},{6,10},{... | collective-permute-start | bytes 983048 | tf_op jit(solution)/shard_map/ppermute | solution.py:156
  123.3 14.7 %collective-permute-start.3 = (bf16[128,1280]{1,0:T(8,128)(2,1)S(1)}, bf16[128,1280]{1,0:T(8,128)(2,1)S(1)}, u32[]{:S(2)}, u32[]{:S(2)}) collective-permute-start(bf16[128,1280]{1,0:T(8,128)(2,1)S(1)} %broadcast_select_fusion), channel_id=1, source_target_pairs={{0,12},{4,0},{8,4},{12,8},{1,13},{5,1},{9,5},{13,9},{2,14},{6,2},{... | collective-permute-start | bytes 983048 | tf_op jit(solution)/shard_map/ppermute | solution.py:158
Sparse Core Ops, SparseCore 0:
  31.1 55.0 all-gather.3
